TPU v7x, 512 devices: a whole 4x8x8 slice. The times are simulated.
512 devices in a mesh: shard: 128 (over y, z, core), tensor: 4 (over x).
Axes of the slice: x: 4, y: 8, z: 8, core: 2. Of those that a mesh axis runs over, the one named last changes fastest.
Arguments:
- big_grad: bfloat16 [32, 1280, 768], P(None, 'shard', 'tensor')
- big_weight: bfloat16 [32, 1280, 768], P(None, 'shard', 'tensor'), may hold values from -0.017944336 to 0.017944336
- big_moment: float32 [128, 768, 1280], P('shard', 'tensor'), may hold values from -6 to 6
- small_grad: bfloat16 [32, 1280, 192], P(None, 'shard')
- small_weight: bfloat16 [32, 1280, 192], P(None, 'shard'), may hold values from -0.15625 to 0.15625
- small_moment: float32 [128, 192, 1280], P('shard'), may hold values from -6 to 6
- owners: int32 [2, 32], replicated, may hold values from 0 to 127, as said below
- vec_parts: float32 [128, 43008], P('shard'), may hold values from -0.6 to 0.6
- vec_param: float32 [43008], P('shard'), may hold values from 0.5 to 1.5
- vec_first: float32 [43008], P('shard'), may hold values from -0.6 to 0.6
- vec_second: float32 [43008], P('shard'), may hold values from 0.01 to 1
Outputs:
- big_weight_new: bfloat16 [32, 1280, 768], P(None, 'shard', 'tensor')
- big_moment_new: float32 [128, 768, 1280], P('shard', 'tensor')
- small_weight_new: bfloat16 [32, 1280, 192], P(None, 'shard')
- small_moment_new: float32 [128, 192, 1280], P('shard')
- vec_param_new: float32 [43008], P('shard')
- vec_first_new: float32 [43008], P('shard')
- vec_second_new: float32 [43008], P('shard')
Inputs may be any that keep to these rules, and one draw needn't show every extreme that they name: `owners`: no shard index appears twice in the whole list (over both rows); each aligned group of four shard indices holds exactly one owner of each row; the first and the last shard index own a matrix.
All inputs are finite; a program needn't handle non-finite values.
Results may differ from a plain program's by a relative error of at most 0.0068.
Values may be sent and summed in bfloat16 or wider, within the bound.
No kernel may reach another device: no remote copies, remote signals or barrier semaphores. Data moves between devices by JAX's collectives and lax.ppermute only.
A program may use at most 64 MiB of HBM per device.

v0:
```python
import math
import jax
import jax.numpy as jnp
from jax import lax
from jax.sharding import PartitionSpec as P

D = 1280
ITERS = 2
newton_linear = 3.4445
newton_cubic = -4.775
newton_quintic = 2.0315
momentum_rate = 0.95
muon_rate = 0.05
weight_decay = 0.1
norm_epsilon = 1e-07
adam_rate = 0.004
first_decay = 0.9
second_decay = 0.95
adam_epsilon = 1e-08
first_correct = 0.99997343860111
second_correct = 0.99407947077967


def owner_table(owner_list, count):
    devices = lax.broadcasted_iota(jnp.int32, (count, owner_list.shape[0]), 0)
    return (devices == owner_list[None, :]).astype(jnp.bfloat16)


def route_rows(owner_map, pieces):
    flattened = pieces.reshape(pieces.shape[0], -1)
    routed = jnp.dot(owner_map, flattened, preferred_element_type=jnp.float32)
    return routed.astype(jnp.bfloat16).reshape((owner_map.shape[0],) + pieces.shape[1:])


def collect(owner_map, arrived):
    flattened = arrived.reshape(arrived.shape[0], -1)
    picked = lax.dot_general(
        owner_map, flattened, (((0,), (0,)), ((), ())), preferred_element_type=jnp.float32
    )
    return picked.astype(jnp.bfloat16).reshape((owner_map.shape[1],) + arrived.shape[1:])


def advance(arrived, moment, is_owner):
    gradient = arrived.T.astype(jnp.float32)
    renewed = momentum_rate * moment + gradient
    retained = jnp.where(is_owner, renewed, moment)
    blended = jnp.where(is_owner, gradient + momentum_rate * renewed, 0.0).astype(jnp.bfloat16).T
    return (retained, blended)


def normalized(field):
    values = field.astype(jnp.float32)
    squares = jnp.sum(values * values)
    return (values / (jnp.sqrt(squares) + norm_epsilon)).astype(jnp.bfloat16)


def gram_block(left_part, right_part):
    product = lax.dot_general(
        left_part, right_part, (((0,), (0,)), ((), ())), preferred_element_type=jnp.float32
    )
    return product.astype(jnp.bfloat16)


def poly_block(gram_part, gram_full):
    square = jnp.dot(gram_part, gram_full, preferred_element_type=jnp.float32)
    return (newton_cubic * gram_part.astype(jnp.float32) + newton_quintic * square).astype(
        jnp.bfloat16
    )


def newton_step(column_part, full_iterate, polynomial):
    product = lax.dot_general(
        full_iterate, polynomial, (((1,), (1,)), ((), ())), preferred_element_type=jnp.float32
    )
    return (newton_linear * column_part.astype(jnp.float32) + product).astype(jnp.bfloat16)


def small_newton(field):
    iterate = normalized(field)
    for iteration in range(ITERS):
        gram_full = gram_block(iterate, iterate)
        iterate = newton_step(iterate, iterate, poly_block(gram_full, gram_full))
    return iterate


def apply_update(weight, update):
    scale = 0.2 * math.sqrt(D)
    values = weight.astype(jnp.float32)
    return (
        values - muon_rate * (scale * update.astype(jnp.float32) + weight_decay * values)
    ).astype(jnp.bfloat16)


def gather_columns(column_part):
    return lax.all_gather(column_part, "tensor", axis=1, tiled=True)


def gather_gram(gram_part):
    return lax.all_gather(gram_part, "tensor", axis=0, tiled=True)


def per_device(
    big_grad,
    big_weight,
    big_moment,
    small_grad,
    small_weight,
    small_moment,
    owners,
    vec_parts,
    vec_param,
    vec_first,
    vec_second,
):
    shards = lax.axis_size("shard")
    shard_place = lax.axis_index("shard")
    column = lax.axis_index("tensor")
    block_width = big_grad.shape[2]
    rows_dev = big_grad.shape[1]
    matrices = big_grad.shape[0]
    joint_map = owner_table(jnp.concatenate([owners[0], owners[1]]), shards)
    joint_pieces = jnp.concatenate([big_grad, small_grad], axis=0)
    arrived = lax.all_to_all(
        route_rows(joint_map, joint_pieces), "shard", split_axis=0, concat_axis=1, tiled=True
    )[0]
    big_owner = jnp.any(owners[0] == shard_place)
    small_owner = jnp.any(owners[1] == shard_place)
    big_retained, big_blended = advance(arrived, big_moment[0], big_owner)
    small_retained, small_blended = advance(arrived, small_moment[0], small_owner)
    small_result = small_newton(small_blended)
    full_iterate = normalized(gather_columns(big_blended))
    for iteration in range(ITERS):
        owned_part = lax.dynamic_slice_in_dim(full_iterate, column * block_width, block_width, 1)
        gram_full = gather_gram(gram_block(owned_part, full_iterate))
        full_iterate = newton_step(full_iterate, full_iterate, poly_block(gram_full, gram_full))
    big_result = lax.dynamic_slice_in_dim(full_iterate, column * block_width, block_width, 1)
    own_result = jnp.where(big_owner, big_result, small_result)
    returned = lax.all_to_all(
        own_result.reshape(shards, rows_dev, block_width),
        "shard",
        split_axis=0,
        concat_axis=0,
        tiled=True,
    )
    picked = collect(joint_map, returned)
    big_weight_new = apply_update(big_weight, picked[:matrices])
    small_weight_new = apply_update(small_weight, picked[matrices:])
    grad_share = lax.psum_scatter(vec_parts[0], "shard", scatter_dimension=0, tiled=True)
    first_new = first_decay * vec_first + (1.0 - first_decay) * grad_share
    second_new = second_decay * vec_second + (1.0 - second_decay) * grad_share * grad_share
    param_new = vec_param - adam_rate * (first_new / first_correct) / (
        jnp.sqrt(second_new / second_correct) + adam_epsilon
    )
    return (
        big_weight_new,
        big_retained[None],
        small_weight_new,
        small_retained[None],
        param_new,
        first_new,
        second_new,
    )


def solution(mesh):
    return jax.shard_map(
        per_device,
        mesh=mesh,
        in_specs=(
            P(None, "shard", "tensor"),
            P(None, "shard", "tensor"),
            P("shard", "tensor", None),
            P(None, "shard", None),
            P(None, "shard", None),
            P("shard", None, None),
            P(),
            P("shard", None),
            P("shard"),
            P("shard"),
            P("shard"),
        ),
        out_specs=(
            P(None, "shard", "tensor"),
            P("shard", "tensor", None),
            P(None, "shard", None),
            P("shard", None, None),
            P("shard"),
            P("shard"),
            P("shard"),
        ),
        check_vma=False,
    )
```

profile of v0, /device:TPU:1, one launch (start us, length us, event | category | flops | bytes accessed | tf_op | source)
XLA Modules:
  0.0 395.7 jit_solution(8860446382771876976)
XLA Ops:
  8.0 0.8 slice_bitcast_fusion.1
  8.8 1.0 pad_maximum_fusion
  11.0 1.3 copy.34
  12.4 1.6 reshape.48
  13.9 18.4 %all-to-all-start = ((bf16[128,2,960]{2,1,0:T(2,128)(2,1)}), bf16[128,2,960]{2,1,0:T(2,128)(2,1)S(1)}, u32[]{:S(2)}, u32[]{:S(2)}) async-start(bf16[128,2,960]{2,1,0:T(2,128)(2,1)} %reshape.48), calls=%async_computation | async-start | bytes 1048576 | tf_op jit(solution)/shard_map/all_to_all | solution.py:123
  32.4 0.6 compare_reduce_fusion.1
  33.1 18.7 %all-to-all-done = bf16[128,2,960]{2,1,0:T(2,128)(2,1)S(1)} async-done(((bf16[128,2,960]{2,1,0:T(2,128)(2,1)}), bf16[128,2,960]{2,1,0:T(2,128)(2,1)S(1)}, u32[]{:S(2)}, u32[]{:S(2)}) %all-to-all-start) | async-done | bytes 491552 | tf_op jit(solution)/shard_map/all_to_all | solution.py:123
  51.8 0.8 reshape.49
  52.9 0.4 copy.35
  53.3 0.8 copy-done.2
  54.1 4.9 %fusion.15 = (f32[1,192,1280]{2,1,0:T(8,128)}, bf16[1280,192]{0,1:T(8,128)(2,1)}, f32[1,192,1280]{2,1,0:T(8,128)}, f32[]{:T(128)}, bf16[192,1280]{1,0:T(8,128)(2,1)S(1)}) fusion(f32[1,192,1280]{2,1,0:T(8,128)S(1)} %copy-done.2, f32[1280,192]{0,1:T(8,128)S(1)} %copy.35, pred[]{:T(512)} %get-tuple-element.21, f32[1,192,1280]{2,1,0:T(8,128)} %param.16, ...), kind=kLoop, calls=%fused_computation.37 | loop fusion | flops 4177919 | bytes 5898246 | tf_op jit(solution)/shard_map/broadcast_in_dim | solution.py:156
  59.0 28.6 %all-gather.4.cloned.1.call-done = bf16[1280,768]{0,1:T(8,128)(2,1)} async-done(((bf16[1280,192]{0,1:T(8,128)(2,1)}), bf16[1280,768]{0,1:T(8,128)(2,1)}) %all-gather.4.cloned.1.call-update) | async-done | bytes 1966096 | tf_op jit(solution)/shard_map/all_gather | solution.py:95
  87.6 3.3 fusion
  92.0 1.3 copy-done.1
  93.3 1.5 convolution_convert_fusion.3
  95.1 27.7 %all-gather.6.cloned.1.call-done = bf16[768,768]{1,0:T(8,128)(2,1)} async-done(((bf16[192,768]{1,0:T(8,128)(2,1)}), bf16[768,768]{1,0:T(8,128)(2,1)}) %all-gather.6.cloned.1.call-update) | async-done | bytes 1179664 | tf_op jit(solution)/shard_map/all_gather | solution.py:99
  122.8 6.0 %add_convert_fusion = bf16[1280,768]{0,1:T(8,128)(2,1)S(1)} fusion(bf16[1280,768]{0,1:T(8,128)(2,1)} %copy-done.1, bf16[768,768]{1,0:T(8,128)(2,1)} %all-gather.6.cloned.1.call-done), kind=kOutput, calls=%fused_computation.4 | convolution fusion | flops 2422800384 | bytes 5111808 | tf_op jit(solution)/shard_map/dot_general | solution.py:72
  128.8 1.5 convolution_convert_fusion.2
  131.4 0.5 fusion.2
  132.2 28.7 %all-gather.8.cloned.1.call-done = bf16[768,768]{1,0:T(8,128)(2,1)} async-done(((bf16[192,768]{1,0:T(8,128)(2,1)}), bf16[768,768]{1,0:T(8,128)(2,1)}) %all-gather.8.cloned.1.call-update) | async-done | bytes 1179664 | tf_op jit(solution)/shard_map/all_gather | solution.py:99
  160.8 7.5 %fusion.20 = f32[1280,768]{0,1:T(8,128)} fusion(bf16[1280,768]{0,1:T(8,128)(2,1)} %copy-done.9, bf16[768,768]{1,0:T(8,128)(2,1)} %all-gather.8.cloned.1.call-done), kind=kOutput, calls=%fused_computation.44 | convolution fusion | flops 2418868224 | bytes 7077888 | tf_op jit(solution)/shard_map/dot_general | solution.py:72
  168.3 2.4 fusion.4
  171.3 1.6 reshape.50
  172.9 16.4 %all-to-all-start.1 = ((bf16[128,2,960]{2,1,0:T(2,128)(2,1)}), bf16[128,2,960]{2,1,0:T(2,128)(2,1)S(1)}, u32[]{:S(2)}, u32[]{:S(2)}) async-start(bf16[128,2,960]{2,1,0:T(2,128)(2,1)} %reshape.50), calls=%async_computation.1 | async-start | bytes 1048576 | tf_op jit(solution)/shard_map/all_to_all | solution.py:138
  189.4 0.5 all-reduce.3.cloned.1.call-update
  189.9 1.3 dynamic-slice
  191.8 191.3 %all-reduce.3.cloned.1.call-done = f32[43008]{0:T(1024)} async-done(((f32[43008]{0:T(1024)}), f32[43008]{0:T(1024)}) %all-reduce.3.cloned.1.call-update) | async-done | bytes 172048
  383.2 1.4 divide_subtract_fusion
  384.5 0.8 reshape.51
  385.3 0.7 copy.37
  386.8 0.7 copy.39
  387.9 0.7 copy.40
  (43 shorter events, 4.5 us)
Async XLA Ops:
  11.0 21.4 %copy-start.5 = (s32[2,32]{1,0:T(2,128)S(1)}, s32[2,32]{1,0:T(2,128)}, u32[]{:S(2)}) copy-start(s32[2,32]{1,0:T(2,128)} %param.17) | copy-start | bytes 772
  13.9 37.8 %all-to-all-start = ((bf16[128,2,960]{2,1,0:T(2,128)(2,1)}), bf16[128,2,960]{2,1,0:T(2,128)(2,1)S(1)}, u32[]{:S(2)}, u32[]{:S(2)}) async-start(bf16[128,2,960]{2,1,0:T(2,128)(2,1)} %reshape.48), calls=%async_computation | async-start | bytes 1048576 | tf_op jit(solution)/shard_map/all_to_all | solution.py:123
  32.4 55.2 %all-gather.4.cloned.1.call-start = ((), (), s32[]{:S(2)}) async-start(), calls=%async_computation.2 | async-start | bytes 2457600 | tf_op jit(solution)/shard_map/all_gather | solution.py:95
  52.9 1.2 copy-start.2
  59.0 63.8 %all-gather.6.cloned.1.call-start = ((), (), s32[]{:S(2)}) async-start(), calls=%async_computation.3 | async-start | bytes 1474560 | tf_op jit(solution)/shard_map/all_gather | solution.py:99
  87.6 4.0 %copy-start = (bf16[1280,768]{0,1:T(8,128)(2,1)S(1)}, bf16[1280,768]{0,1:T(8,128)(2,1)}, u32[]{:S(2)}) copy-start(bf16[1280,768]{0,1:T(8,128)(2,1)} %all-gather.4.cloned.1.call-done) | copy-start | bytes 5898244
  92.0 1.3 copy-start.1
  94.8 66.0 %all-gather.8.cloned.1.call-start = ((), (), s32[]{:S(2)}) async-start(), calls=%async_computation.4 | async-start | bytes 1474560 | tf_op jit(solution)/shard_map/all_gather | solution.py:99
  128.8 2.3 copy-start.9
  171.0 212.1 %copy-start.6 = (f32[336]{0:T(512)S(1)}, f32[336]{0:T(512)}, u32[]{:S(2)}) copy-start(f32[336]{0:T(512)} %param.19) | copy-start | bytes 4036
  171.0 212.1 %copy-start.7 = (f32[336]{0:T(512)S(1)}, f32[336]{0:T(512)}, u32[]{:S(2)}) copy-start(f32[336]{0:T(512)} %param.20) | copy-start | bytes 4036
  171.1 212.1 %copy-start.8 = (f32[336]{0:T(512)S(1)}, f32[336]{0:T(512)}, u32[]{:S(2)}) copy-start(f32[336]{0:T(512)} %param.21) | copy-start | bytes 4036
  172.9 211.6 %all-to-all-start.1 = ((bf16[128,2,960]{2,1,0:T(2,128)(2,1)}), bf16[128,2,960]{2,1,0:T(2,128)(2,1)S(1)}, u32[]{:S(2)}, u32[]{:S(2)}) async-start(bf16[128,2,960]{2,1,0:T(2,128)(2,1)} %reshape.50), calls=%async_computation.1 | async-start | bytes 1048576 | tf_op jit(solution)/shard_map/all_to_all | solution.py:138
  189.3 193.8 %all-reduce.3.cloned.1.call-start = ((), (), s32[]{:S(2)}) async-start(), calls=%async_computation.5 | async-start | bytes 344064
  385.3 1.3 copy-start.3
  386.4 1.3 copy-start.4
Sparse Core Ops, SparseCore 0:
  59.1 28.4 all-gather.3
  94.9 27.7 all-gather.5
  130.5 30.3 all-gather.7
Sparse Core Ops, SparseCore 1:
  193.0 190.0 all-reduce.2
where the time goes:
time: 396 us
  waiting for transfers between devices  296 us (75%)
  starting transfers between devices  35.2 us (9%)
  matrix products  20.7 us (5%)
  between operations  17.5 us (4%)
  local copies, waits for them, and re-layouts  14.7 us (4%)
  other arithmetic  12 us (3%)
    unnamed x5, waiting for transfers between devices  192 us
    all_gather x2, waiting for transfers between devices, gather_gram(): return lax.all_gather(gram_part, 'tensor', axis=0, tiled=True)  56.4 us
    all_gather x1, waiting for transfers between devices, gather_columns(): return lax.all_gather(column_part, 'tensor', axis=1, tiled=True)  28.6 us
    all_to_all x1, waiting for transfers between devices, per_device(): lax.all_to_all(route_rows(joint_map, joint_pieces), 'shard', split_axis=0...  18.7 us
    all_to_all x1, starting transfers between devices, per_device(): lax.all_to_all(route_rows(joint_map, joint_pieces), 'shard', split_axis=0...  18.4 us
    dot_general x4, matrix products, newton_step(): lax.dot_general(full_iterate, polynomial, (((1,), (1,)), ((), ())), prefe...  16.4 us
    all_to_all x1, starting transfers between devices, per_device(): lax.all_to_all(own_result.reshape(shards, rows_dev, block_width), 'shard'...  16.4 us
    unnamed x27, local copies, waits for them, and re-layouts  9.48 us
  transfers between devices with their start and end apart: 6, of which 5 were waited for; matrix products, arithmetic and copies ran while one was open for 1% of the time, Pallas kernels for 0%

commit v1 on v0

--- a/solution.py
+++ b/solution.py
@@ -21,6 +21,24 @@
 second_correct = 0.99407947077967
 
 
+def gather_around(array, axis, dim):
+    ways, here, step = (lax.axis_size(axis), lax.axis_index(axis), array.shape[dim])
+    shape = [n * ways if d == dim else n for d, n in enumerate(array.shape)]
+    full = lax.dynamic_update_slice_in_dim(
+        jnp.zeros(shape, array.dtype), array, here * step, axis=dim
+    )
+    going_up = going_down = array
+    for far in range(1, ways // 2 + 1):
+        going_up = lax.ppermute(going_up, axis, [(d, (d + 1) % ways) for d in range(ways)])
+        full = lax.dynamic_update_slice_in_dim(full, going_up, (here - far) % ways * step, axis=dim)
+        if 2 * far < ways:
+            going_down = lax.ppermute(going_down, axis, [(d, (d - 1) % ways) for d in range(ways)])
+            full = lax.dynamic_update_slice_in_dim(
+                full, going_down, (here + far) % ways * step, axis=dim
+            )
+    return full
+
+
 def owner_table(owner_list, count):
     devices = lax.broadcasted_iota(jnp.int32, (count, owner_list.shape[0]), 0)
     return (devices == owner_list[None, :]).astype(jnp.bfloat16)
@@ -96,7 +114,7 @@
 
 
 def gather_gram(gram_part):
-    return lax.all_gather(gram_part, "tensor", axis=0, tiled=True)
+    return gather_around(gram_part, "tensor", 0)
 
 
 def per_device(

time: 396 us -> 374 us (0.944)
  waiting for transfers between devices: 296 us -> 256 us
  starting transfers between devices: 35.2 us -> 53.9 us
    all_gather x2 -> x0, waiting for transfers between devices: 56.4 us -> none  [gather_gram(): return lax.all_gather(gram_part, 'tensor', axis=0, tiled=True)]
    ppermute x0 -> x6, waiting for transfers between devices: none -> 18.4 us  [the longest x4 18.4 us: gather_around(): lax.ppermute(going_up, axis, [(d, (d + 1) % ways) for d in range(ways)])]
    ppermute x0 -> x6, starting transfers between devices: none -> 17 us  [the longest x2 8.93 us: gather_around(): lax.ppermute(going_down, axis, [(d, (d - 1) % ways) for d in range(ways)])]
    unnamed x5 -> x3, waiting for transfers between devices: 192 us -> 190 us
    unnamed x27 -> x29, local copies, waits for them, and re-layouts: 9.48 us -> 7.84 us
  transfers between devices with their start and end apart: 6 -> 10, of which waited for: 5 -> 7; matrix products, arithmetic and copies ran while one was open for 1% -> 2% of each run, Pallas kernels for 0% -> 0%
where the time goes in v1:
time: 374 us; the launch traced here: 373 us
  waiting for transfers between devices  256 us (68%)
  starting transfers between devices  53.9 us (14%)
  matrix products  19.9 us (5%)
  between operations  18 us (5%)
  local copies, waits for them, and re-layouts  13.4 us (4%)
  other arithmetic  12.2 us (3%)
    unnamed x3, waiting for transfers between devices  190 us
    all_gather x1, waiting for transfers between devices, gather_columns(): return lax.all_gather(column_part, 'tensor', axis=1, tiled=True)  28.6 us
    all_to_all x1, waiting for transfers between devices, per_device(): lax.all_to_all(route_rows(joint_map, joint_pieces), 'shard', split_axis=0...  18.7 us
    all_to_all x1, starting transfers between devices, per_device(): lax.all_to_all(route_rows(joint_map, joint_pieces), 'shard', split_axis=0...  18.4 us
    ppermute x4, waiting for transfers between devices, gather_around(): lax.ppermute(going_up, axis, [(d, (d + 1) % ways) for d in range(ways)])  18.4 us
    all_to_all x1, starting transfers between devices, per_device(): lax.all_to_all(own_result.reshape(shards, rows_dev, block_width), 'shard'...  18.2 us
    dot_general x4, matrix products, newton_step(): lax.dot_general(full_iterate, polynomial, (((1,), (1,)), ((), ())), prefe...  13.2 us
    ppermute x2, starting transfers between devices, gather_around(): lax.ppermute(going_down, axis, [(d, (d - 1) % ways) for d in range(ways)])  8.93 us
  transfers between devices with their start and end apart: 10, of which 7 were waited for; matrix products, arithmetic and copies ran while one was open for 2% of the time, Pallas kernels for 0%

profile of v1, /device:TPU:1, one launch (start us, length us, event | category | flops | bytes accessed | tf_op | source)
XLA Modules:
  0.0 373.0 jit_solution(8198781889230696485)
XLA Ops:
  8.0 0.8 slice_bitcast_fusion.1
  8.8 1.0 pad_maximum_fusion
  11.0 1.3 copy.34
  12.4 1.6 reshape.48
  13.9 18.4 %all-to-all-start = ((bf16[128,2,960]{2,1,0:T(2,128)(2,1)}), bf16[128,2,960]{2,1,0:T(2,128)(2,1)S(1)}, u32[]{:S(2)}, u32[]{:S(2)}) async-start(bf16[128,2,960]{2,1,0:T(2,128)(2,1)} %reshape.48), calls=%async_computation | async-start | bytes 1048576 | tf_op jit(solution)/shard_map/all_to_all | solution.py:141
  33.1 18.7 %all-to-all-done = bf16[128,2,960]{2,1,0:T(2,128)(2,1)S(1)} async-done(((bf16[128,2,960]{2,1,0:T(2,128)(2,1)}), bf16[128,2,960]{2,1,0:T(2,128)(2,1)S(1)}, u32[]{:S(2)}, u32[]{:S(2)}) %all-to-all-start) | async-done | bytes 491552 | tf_op jit(solution)/shard_map/all_to_all | solution.py:141
  51.8 0.8 reshape.49
  53.7 5.0 %fusion.15 = (f32[1,192,1280]{2,1,0:T(8,128)}, bf16[1280,192]{0,1:T(8,128)(2,1)}, f32[1,192,1280]{2,1,0:T(8,128)}, f32[]{:T(128)}, bf16[192,1280]{1,0:T(8,128)(2,1)}) fusion(f32[1,192,1280]{2,1,0:T(8,128)S(1)} %copy-done.3, f32[1280,192]{0,1:T(8,128)S(1)} %copy.35, pred[]{:T(512)} %get-tuple-element.21, f32[1,192,1280]{2,1,0:T(8,128)} %param.16, ...), kind=kLoop, calls=%fused_computation.37 | loop fusion | flops 4177919 | bytes 5898246 | tf_op jit(solution)/shard_map/broadcast_in_dim | solution.py:174
  58.8 28.6 %all-gather.2.cloned.1.call-done = bf16[1280,768]{0,1:T(8,128)(2,1)} async-done(((bf16[1280,192]{0,1:T(8,128)(2,1)}), bf16[1280,768]{0,1:T(8,128)(2,1)}) %all-gather.2.cloned.1.call-update) | async-done | bytes 1966096 | tf_op jit(solution)/shard_map/all_gather | solution.py:113
  87.4 3.3 fusion
  91.9 1.5 constant_dynamic-update-slice_fusion.7
  93.4 2.1 collective-permute-start
  96.3 4.4 %collective-permute-start.1 = (bf16[192,768]{1,0:T(8,128)(2,1)}, bf16[192,768]{1,0:T(8,128)(2,1)S(1)}, u32[]{:S(2)}, u32[]{:S(2)}) collective-permute-start(bf16[192,768]{1,0:T(8,128)(2,1)} %get-tuple-element.39), channel_id=1, source_target_pairs={{0,3},{1,0},{2,1},{3,2},{4,7},{5,4},{6,5},{7,6},{8,11},{9,8},{10,9... | collective-permute-start | bytes 884744 | tf_op jit(solution)/shard_map/ppermute | solution.py:35
  100.6 3.8 %collective-permute-done = bf16[192,768]{1,0:T(8,128)(2,1)S(1)} collective-permute-done((bf16[192,768]{1,0:T(8,128)(2,1)}, bf16[192,768]{1,0:T(8,128)(2,1)S(1)}, u32[]{:S(2)}, u32[]{:S(2)}) %collective-permute-start) | collective-permute-done | bytes 294944 | tf_op jit(solution)/shard_map/ppermute | solution.py:32
  104.4 2.1 collective-permute-start.2
  106.5 1.7 convolution_convert_fusion.5
  108.3 6.1 %collective-permute-done.2 = bf16[192,768]{1,0:T(8,128)(2,1)S(1)} collective-permute-done((bf16[192,768]{1,0:T(8,128)(2,1)S(1)}, bf16[192,768]{1,0:T(8,128)(2,1)S(1)}, u32[]{:S(2)}, u32[]{:S(2)}) %collective-permute-start.2) | collective-permute-done | bytes 294944 | tf_op jit(solution)/shard_map/ppermute | solution.py:32
  114.4 4.1 %add_convert_fusion = bf16[1280,768]{0,1:T(8,128)(2,1)} fusion(bf16[1280,768]{0,1:T(8,128)(2,1)S(1)} %copy-done.2, bf16[768,768]{1,0:T(8,128)(2,1)S(1)} %constant_dynamic-update-slice_fusion.4), kind=kOutput, calls=%fused_computation.4 | convolution fusion | flops 2422800384 | bytes 5111808 | tf_op jit(solution)/shard_map/dot_general | solution.py:90
  118.6 2.6 constant_dynamic-update-slice_fusion.3
  121.2 1.9 collective-permute-start.3
  123.6 4.6 %collective-permute-start.4 = (bf16[192,768]{1,0:T(8,128)(2,1)S(1)}, bf16[192,768]{1,0:T(8,128)(2,1)S(1)}, u32[]{:S(2)}, u32[]{:S(2)}) collective-permute-start(bf16[192,768]{1,0:T(8,128)(2,1)S(1)} %get-tuple-element.41), channel_id=1, source_target_pairs={{0,3},{1,0},{2,1},{3,2},{4,7},{5,4},{6,5},{7,6},{8,11},{9,8},{10,9... | collective-permute-start | bytes 884744 | tf_op jit(solution)/shard_map/ppermute | solution.py:35
  128.1 2.1 collective-permute-done.3
  130.3 1.9 collective-permute-start.5
  132.6 6.4 %collective-permute-done.5 = bf16[192,768]{1,0:T(8,128)(2,1)S(1)} collective-permute-done((bf16[192,768]{1,0:T(8,128)(2,1)S(1)}, bf16[192,768]{1,0:T(8,128)(2,1)S(1)}, u32[]{:S(2)}, u32[]{:S(2)}) %collective-permute-start.5) | collective-permute-done | bytes 294944 | tf_op jit(solution)/shard_map/ppermute | solution.py:32
  139.0 6.2 %fusion.20 = f32[1280,768]{0,1:T(8,128)} fusion(bf16[1280,768]{0,1:T(8,128)(2,1)} %add_convert_fusion, bf16[768,768]{1,0:T(8,128)(2,1)S(1)} %constant_dynamic-update-slice_fusion), kind=kOutput, calls=%fused_computation.44 | convolution fusion | flops 2418868224 | bytes 7077888 | tf_op jit(solution)/shard_map/dot_general | solution.py:90
  145.2 2.4 fusion.4
  148.2 1.6 reshape.50
  149.8 18.2 %all-to-all-start.1 = ((bf16[128,2,960]{2,1,0:T(2,128)(2,1)}), bf16[128,2,960]{2,1,0:T(2,128)(2,1)S(1)}, u32[]{:S(2)}, u32[]{:S(2)}) async-start(bf16[128,2,960]{2,1,0:T(2,128)(2,1)} %reshape.50), calls=%async_computation.1 | async-start | bytes 1048576 | tf_op jit(solution)/shard_map/all_to_all | solution.py:156
  168.5 1.3 dynamic-slice
  170.4 189.6 %all-reduce.3.cloned.1.call-done = f32[43008]{0:T(1024)} async-done(((f32[43008]{0:T(1024)}), f32[43008]{0:T(1024)}) %all-reduce.3.cloned.1.call-update) | async-done | bytes 172048
  360.1 1.4 divide_subtract_fusion
  361.5 0.8 reshape.51
  (59 shorter events, 8.8 us)
Async XLA Ops:
  11.0 21.4 %copy-start.7 = (s32[2,32]{1,0:T(2,128)S(1)}, s32[2,32]{1,0:T(2,128)}, u32[]{:S(2)}) copy-start(s32[2,32]{1,0:T(2,128)} %param.17) | copy-start | bytes 772
  13.9 37.8 %all-to-all-start = ((bf16[128,2,960]{2,1,0:T(2,128)(2,1)}), bf16[128,2,960]{2,1,0:T(2,128)(2,1)S(1)}, u32[]{:S(2)}, u32[]{:S(2)}) async-start(bf16[128,2,960]{2,1,0:T(2,128)(2,1)} %reshape.48), calls=%async_computation | async-start | bytes 1048576 | tf_op jit(solution)/shard_map/all_to_all | solution.py:141
  32.4 55.0 %all-gather.2.cloned.1.call-start = ((), (), s32[]{:S(2)}) async-start(), calls=%async_computation.2 | async-start | bytes 2457600 | tf_op jit(solution)/shard_map/all_gather | solution.py:113
  52.5 1.2 copy-start.3
  87.4 4.0 %copy-start = (bf16[1280,768]{0,1:T(8,128)(2,1)S(1)}, bf16[1280,768]{0,1:T(8,128)(2,1)}, u32[]{:S(2)}) copy-start(bf16[1280,768]{0,1:T(8,128)(2,1)} %all-gather.2.cloned.1.call-done) | copy-start | bytes 5898244
  91.8 1.6 copy-start.1
  93.4 11.0 %collective-permute-start = (bf16[192,768]{1,0:T(8,128)(2,1)}, bf16[192,768]{1,0:T(8,128)(2,1)S(1)}, u32[]{:S(2)}, u32[]{:S(2)}) collective-permute-start(bf16[192,768]{1,0:T(8,128)(2,1)} %get-tuple-element.39), channel_id=1, source_target_pairs={{0,1},{1,2},{2,3},{3,0},{4,5},{5,6},{6,7},{7,4},{8,9},{9,10},{10,1... | collective-permute-start | bytes 884744 | tf_op jit(solution)/shard_map/ppermute | solution.py:32
  96.3 12.0 %collective-permute-start.1 = (bf16[192,768]{1,0:T(8,128)(2,1)}, bf16[192,768]{1,0:T(8,128)(2,1)S(1)}, u32[]{:S(2)}, u32[]{:S(2)}) collective-permute-start(bf16[192,768]{1,0:T(8,128)(2,1)} %get-tuple-element.39), channel_id=1, source_target_pairs={{0,3},{1,0},{2,1},{3,2},{4,7},{5,4},{6,5},{7,6},{8,11},{9,8},{10,9... | collective-permute-start | bytes 884744 | tf_op jit(solution)/shard_map/ppermute | solution.py:35
  104.4 10.0 %collective-permute-start.2 = (bf16[192,768]{1,0:T(8,128)(2,1)S(1)}, bf16[192,768]{1,0:T(8,128)(2,1)S(1)}, u32[]{:S(2)}, u32[]{:S(2)}) collective-permute-start(bf16[192,768]{1,0:T(8,128)(2,1)S(1)} %collective-permute-done), channel_id=1, source_target_pairs={{0,1},{1,2},{2,3},{3,0},{4,5},{5,6},{6,7},{7,4},{8,9},{9,10},{10,1... | collective-permute-start | bytes 884744 | tf_op jit(solution)/shard_map/ppermute | solution.py:32
  106.5 7.9 %copy-start.2 = (bf16[1280,768]{0,1:T(8,128)(2,1)S(1)}, bf16[1280,768]{0,1:T(8,128)(2,1)}, u32[]{:S(2)}) copy-start(bf16[1280,768]{0,1:T(8,128)(2,1)} %copy-done.1) | copy-start | bytes 5898244
  118.5 4.6 %copy-start.4 = (bf16[192,1280]{1,0:T(8,128)(2,1)S(1)}, bf16[192,1280]{1,0:T(8,128)(2,1)}, u32[]{:S(2)}) copy-start(bf16[192,1280]{1,0:T(8,128)(2,1)} %get-tuple-element.33) | copy-start | bytes 1474564
  121.2 9.1 %collective-permute-start.3 = (bf16[192,768]{1,0:T(8,128)(2,1)S(1)}, bf16[192,768]{1,0:T(8,128)(2,1)S(1)}, u32[]{:S(2)}, u32[]{:S(2)}) collective-permute-start(bf16[192,768]{1,0:T(8,128)(2,1)S(1)} %get-tuple-element.41), channel_id=1, source_target_pairs={{0,1},{1,2},{2,3},{3,0},{4,5},{5,6},{6,7},{7,4},{8,9},{9,10},{10,1... | collective-permute-start | bytes 884744 | tf_op jit(solution)/shard_map/ppermute | solution.py:32
  123.6 9.0 %collective-permute-start.4 = (bf16[192,768]{1,0:T(8,128)(2,1)S(1)}, bf16[192,768]{1,0:T(8,128)(2,1)S(1)}, u32[]{:S(2)}, u32[]{:S(2)}) collective-permute-start(bf16[192,768]{1,0:T(8,128)(2,1)S(1)} %get-tuple-element.41), channel_id=1, source_target_pairs={{0,3},{1,0},{2,1},{3,2},{4,7},{5,4},{6,5},{7,6},{8,11},{9,8},{10,9... | collective-permute-start | bytes 884744 | tf_op jit(solution)/shard_map/ppermute | solution.py:35
  130.3 8.7 %collective-permute-start.5 = (bf16[192,768]{1,0:T(8,128)(2,1)S(1)}, bf16[192,768]{1,0:T(8,128)(2,1)S(1)}, u32[]{:S(2)}, u32[]{:S(2)}) collective-permute-start(bf16[192,768]{1,0:T(8,128)(2,1)S(1)} %collective-permute-done.3), channel_id=1, source_target_pairs={{0,1},{1,2},{2,3},{3,0},{4,5},{5,6},{6,7},{7,4},{8,9},{9,10},{10,1... | collective-permute-start | bytes 884744 | tf_op jit(solution)/shard_map/ppermute | solution.py:32
  147.9 212.2 %copy-start.8 = (f32[336]{0:T(512)S(1)}, f32[336]{0:T(512)}, u32[]{:S(2)}) copy-start(f32[336]{0:T(512)} %param.19) | copy-start | bytes 4036
  147.9 212.2 %copy-start.9 = (f32[336]{0:T(512)S(1)}, f32[336]{0:T(512)}, u32[]{:S(2)}) copy-start(f32[336]{0:T(512)} %param.20) | copy-start | bytes 4036
  147.9 212.2 %copy-start.10 = (f32[336]{0:T(512)S(1)}, f32[336]{0:T(512)}, u32[]{:S(2)}) copy-start(f32[336]{0:T(512)} %param.21) | copy-start | bytes 4036
  149.8 211.7 %all-to-all-start.1 = ((bf16[128,2,960]{2,1,0:T(2,128)(2,1)}), bf16[128,2,960]{2,1,0:T(2,128)(2,1)S(1)}, u32[]{:S(2)}, u32[]{:S(2)}) async-start(bf16[128,2,960]{2,1,0:T(2,128)(2,1)} %reshape.50), calls=%async_computation.1 | async-start | bytes 1048576 | tf_op jit(solution)/shard_map/all_to_all | solution.py:156
  167.9 192.1 %all-reduce.3.cloned.1.call-start = ((), (), s32[]{:S(2)}) async-start(), calls=%async_computation.3 | async-start | bytes 344064
  362.2 1.3 copy-start.5
  363.3 1.3 copy-start.6
Sparse Core Ops, SparseCore 0:
  58.9 28.4 all-gather.1
Sparse Core Ops, SparseCore 1:
  171.7 188.3 all-reduce.2
